TPU v7x, 32 devices: a whole 2x2x4 slice. The times are simulated.
32 devices in a mesh: lon: 8 (over y, x, core), lat: 4 (over z).
Axes of the slice: x: 2, y: 2, z: 4, core: 2. Of those that a mesh axis runs over, the one named last changes fastest.
Arguments:
- obs_rows: bfloat16 [131072, 128], P(('lon', 'lat')), may hold values from -6 to 6
- cell_ids: int32 [131072], P(('lon', 'lat')), may hold values from 0 to 511
- counts: int32 [32, 32], P(('lon', 'lat')), may hold values from 16 to 128, as said below
- w_embed: bfloat16 [128, 256], replicated, may hold values from -0.5 to 0.5
- w_density: bfloat16 [256], replicated, may hold values from -3 to 3
- kernels: bfloat16 [3, 3, 3, 256, 256], replicated, may hold values from -0.125 to 0.125
- cotangent: bfloat16 [64, 256, 256], P('lat', 'lon'), may hold values from -6 to 6
Outputs:
- encoded: bfloat16 [64, 256, 256], P('lat', 'lon')
- grad_kernels: bfloat16 [3, 3, 3, 256, 256], replicated
- grad_embed: bfloat16 [128, 256], replicated
- grad_obs: bfloat16 [131072, 128], P(('lon', 'lat'))
Inputs may be any that keep to these rules, and one draw needn't show every extreme that they name: `counts`: the live rows of each slot are its first ones; in every draw some tile owner receives 128 live rows from every device.
All inputs are finite; a program needn't handle non-finite values.
Results may differ from a plain program's by a relative error of at most 0.011.
Values may be sent and summed in bfloat16 or wider, within the bound.
No kernel may reach another device: no remote copies, remote signals or barrier semaphores. Data moves between devices by JAX's collectives and lax.ppermute only.
A program may use at most 128 MiB of HBM per device.

v0:
```python
import math

import jax
import jax.numpy as jnp
from jax import lax
from jax.sharding import PartitionSpec as P


def extended(block, sides, width, periodic):
    for axis, dim in sides:
        count = lax.axis_size(axis)
        forward = [(i, i + 1) for i in range(count - 1)]
        if periodic:
            forward.append((count - 1, 0))
        backward = [(target, source) for source, target in forward]
        low = lax.ppermute(
            lax.slice_in_dim(block, block.shape[dim] - width, None, axis=dim), axis, forward
        )
        high = lax.ppermute(lax.slice_in_dim(block, 0, width, axis=dim), axis, backward)
        block = jnp.concatenate([low, block, high], axis=dim)
    return block


def add_rims(field):
    widened = extended(field, (("lon", 1),), 1, True)
    return extended(widened, (("lat", 0),), 1, False)


def conv_valid(padded, kernel):
    return lax.conv_general_dilated(
        padded[None],
        kernel,
        (1, 1),
        "VALID",
        dimension_numbers=("NHWC", "HWIO", "NHWC"),
        preferred_element_type=jnp.float32,
    )[0]


def on_device(obs_rows, cell_ids, counts, w_embed, w_density, kernels, cotangent):
    lon_count = lax.axis_size("lon")
    lat_count = lax.axis_size("lat")
    devices = lon_count * lat_count
    height, tile_width, channels = cotangent.shape
    cell_count = height * tile_width
    slot_rows = obs_rows.shape[0] // devices
    feat_count = obs_rows.shape[1]
    layer_count = kernels.shape[0]
    live_mask = (jnp.arange(slot_rows, dtype=jnp.int32)[None, :] < counts[0][:, None]).reshape(-1)
    sent_ids = jnp.where(live_mask, cell_ids, -1)
    got_rows, got_ids = (
        lax.all_to_all(obs_rows, ("lon", "lat"), split_axis=0, concat_axis=0, tiled=True),
        lax.all_to_all(sent_ids, ("lon", "lat"), split_axis=0, concat_axis=0, tiled=True),
    )
    row_total = got_rows.shape[0]
    block_rows = math.gcd(row_total, 2048)
    cell_iota = jnp.arange(cell_count, dtype=jnp.int32)

    def accumulate(turn_index, running):
        cell_sums, density = running
        begin = turn_index * block_rows
        block_ids = lax.dynamic_slice_in_dim(got_ids, begin, block_rows)
        block_feats = lax.dynamic_slice_in_dim(got_rows, begin, block_rows, 0)
        hit_mask = block_ids[:, None] == cell_iota[None, :]
        onehot = hit_mask.astype(jnp.bfloat16)
        cell_sums = cell_sums + lax.dot_general(
            onehot, block_feats, (((0,), (0,)), ((), ())), preferred_element_type=jnp.float32
        )
        density = density + jnp.sum(hit_mask.astype(jnp.float32), axis=0)
        return (cell_sums, density)

    cell_sums, density = lax.fori_loop(
        0,
        row_total // block_rows,
        accumulate,
        (jnp.zeros((cell_count, feat_count), jnp.float32), jnp.zeros((cell_count,), jnp.float32)),
    )
    inv_root = lax.rsqrt(density + 1.0)
    features = (cell_sums * inv_root[:, None]).astype(jnp.bfloat16)
    start_act = (
        jnp.dot(features, w_embed, preferred_element_type=jnp.float32)
        + jnp.log1p(density)[:, None] * w_density.astype(jnp.float32)[None, :]
    )
    activation = start_act.astype(jnp.bfloat16).reshape(height, tile_width, channels)
    stored_pads = []
    stored_pre = []
    for layer_index in range(layer_count):
        padded = add_rims(activation)
        preact = conv_valid(padded, kernels[layer_index])
        stored_pads.append(padded)
        stored_pre.append(preact)
        activation = (activation.astype(jnp.float32) + jax.nn.silu(preact)).astype(jnp.bfloat16)
    grad_scale = 1.0 / math.sqrt(cell_count * devices)
    back_low = cotangent
    kernel_grads = [None] * layer_count
    for layer_index in reversed(range(layer_count)):
        preact = stored_pre[layer_index]
        sigmoid_v = jax.nn.sigmoid(preact)
        slope_bf = (
            back_low.astype(jnp.float32) * (sigmoid_v * (1.0 + preact * (1.0 - sigmoid_v)))
        ).astype(jnp.bfloat16)
        slope_flat = slope_bf.reshape(cell_count, channels)
        padded = stored_pads[layer_index]
        tap_rows = []
        for row_off in range(3):
            tap_cols = []
            for col_off in range(3):
                window = padded[row_off : row_off + height, col_off : col_off + tile_width].reshape(
                    cell_count, channels
                )
                tap_cols.append(
                    lax.dot_general(
                        window,
                        slope_flat,
                        (((0,), (0,)), ((), ())),
                        preferred_element_type=jnp.float32,
                    )
                )
            tap_rows.append(jnp.stack(tap_cols))
        tap_grad = jnp.stack(tap_rows) * grad_scale
        kernel_grads[layer_index] = tap_grad
        flipped = jnp.transpose(kernels[layer_index][::-1, ::-1], (0, 1, 3, 2))
        spread = conv_valid(add_rims(slope_bf), flipped)
        back_low = lax.optimization_barrier(
            (back_low.astype(jnp.float32) + spread).astype(jnp.bfloat16)
        )
    back_flat = back_low.reshape(cell_count, channels)
    embed_grad = (
        lax.dot_general(
            features, back_flat, (((0,), (0,)), ((), ())), preferred_element_type=jnp.float32
        )
        * grad_scale
    )
    cell_grad = (
        lax.dot_general(
            back_flat, w_embed, (((1,), (1,)), ((), ())), preferred_element_type=jnp.float32
        )
        * inv_root[:, None]
    ).astype(jnp.bfloat16)
    kernel_total, embed_total = lax.psum((jnp.stack(kernel_grads), embed_grad), ("lon", "lat"))
    kernel_out = kernel_total.astype(jnp.bfloat16)
    embed_out = embed_total.astype(jnp.bfloat16)
    picked = jnp.take(cell_grad, jnp.maximum(got_ids, 0), axis=0)
    picked = jnp.where((got_ids >= 0)[:, None], picked, jnp.zeros_like(picked))
    grad_obs = lax.all_to_all(picked, ("lon", "lat"), split_axis=0, concat_axis=0, tiled=True)
    return (activation, kernel_out, embed_out, grad_obs)


def solution(mesh):
    placed = (
        P(("lon", "lat"), None),
        P(("lon", "lat")),
        P(("lon", "lat"), None),
        P(),
        P(),
        P(),
        P("lat", "lon", None),
    )
    return jax.shard_map(
        on_device,
        mesh=mesh,
        in_specs=placed,
        out_specs=(P("lat", "lon", None), P(), P(), P(("lon", "lat"), None)),
        check_vma=False,
    )
```

profile of v0, /device:TPU:0, one launch (start us, length us, event | category | flops | bytes accessed | tf_op | source)
XLA Modules:
  0.0 306.9 jit_solution(6988521680574470004)
XLA Ops:
  0.6 0.8 fusion.102
  1.5 14.3 %all_to_all.33 = s32[32,128,1]{1,2,0:T(1,128)S(1)} all-to-all(s32[32,128,1]{1,2,0:T(1,128)S(1)} %bitcast.270), channel_id=1, replica_groups=mesh['lon'=8,'lat'=4] {'lon','lat'}, dimensions={0} | all-to-all | bytes 32768 | tf_op jit(solution)/shard_map/all_to_all | solution.py:53
  15.7 2.6 all-to-all-start.1
  18.4 0.7 convert_element_type.77
  19.1 24.4 %all-to-all-done.1 = bf16[32,128,128]{2,1,0:T(8,128)(2,1)S(1)} async-done(((bf16[32,128,128]{2,1,0:T(8,128)(2,1)}), bf16[32,128,128]{2,1,0:T(8,128)(2,1)S(1)}, u32[]{:S(2)}, u32[]{:S(2)}) %all-to-all-start.1) | async-done | bytes 1048608 | tf_op jit(solution)/shard_map/all_to_all | solution.py:52
  43.4 4.4 %while.16 = (s32[]{:T(128)}, f32[512,128]{1,0:T(8,128)S(1)}, f32[512]{0:T(512)S(1)}, s32[4096]{0:T(1024)S(1)}, bf16[4096,128]{1,0:T(8,128)(2,1)S(1)}, /*index=5*/s32[]{:T(128)}, s32[]{:T(128)}, s32[]{:T(128)}, s32[]{:T(128)}) while((s32[]{:T(128)}, f32[512,128]{1,0:T(8,128)S(1)}, f32[512]{0:T(512)S(1)}, s32[4096]{0:T(1024)S(1)}, ...), condition=%wide.region_2.3_spmd.clone, body=%wide.region_0.2_spmd.clone.sunk | while | flops 272761344 | bytes 1089702 | solution.py:72
  43.4 0.6 fusion.172
  44.0 1.6 fusion.171
  45.7 0.6 fusion.172
  46.3 1.6 fusion.171
  47.9 0.3 fusion.9
  48.2 1.6 collective-permute-start
  49.9 1.1 collective-permute-start.1
  51.0 1.4 collective-permute-done
  52.4 5.1 %collective-permute-start.2 = (bf16[1,34,256]{2,1,0:T(8,128)(2,1)S(1)}, bf16[1,34,256]{2,1,0:T(8,128)(2,1)S(1)}, u32[]{:S(2)}, u32[]{:S(2)}) collective-permute-start(bf16[1,34,256]{2,1,0:T(8,128)(2,1)S(1)} %get-tuple-element.166), channel_id=1, source_target_pairs={{0,1},{1,2},{2,3},{4,5},{5,6},{6,7},{8,9},{9,10},{10,11},{12,13},{... | collective-permute-start | bytes 52232 | tf_op jit(solution)/shard_map/ppermute | solution.py:16
  57.5 1.3 collective-permute-start.3
  59.0 4.2 %collective-permute-done.3 = bf16[1,34,256]{2,1,0:T(8,128)(2,1)S(1)} collective-permute-done((bf16[1,34,256]{2,1,0:T(8,128)(2,1)S(1)}, bf16[1,34,256]{2,1,0:T(8,128)(2,1)S(1)}, u32[]{:S(2)}, u32[]{:S(2)}) %collective-permute-start.3) | collective-permute-done | bytes 17440 | tf_op jit(solution)/shard_map/ppermute | solution.py:19
  63.7 0.9 convolution_select_fusion.5
  64.9 0.4 add_convert_fusion.2
  65.4 2.6 collective-permute-start.5
  68.0 1.4 collective-permute-done.4
  69.5 1.9 collective-permute-start.6
  71.4 1.3 collective-permute-start.7
  72.8 4.2 %collective-permute-done.7 = bf16[1,34,256]{2,1,0:T(8,128)(2,1)S(1)} collective-permute-done((bf16[1,34,256]{2,1,0:T(8,128)(2,1)S(1)}, bf16[1,34,256]{2,1,0:T(8,128)(2,1)S(1)}, u32[]{:S(2)}, u32[]{:S(2)}) %collective-permute-start.7) | collective-permute-done | bytes 17440 | tf_op jit(solution)/shard_map/ppermute | solution.py:19
  77.5 0.9 convolution_select_fusion.4
  78.7 0.4 add_convert_fusion.1
  79.2 2.6 collective-permute-start.9
  82.0 1.2 collective-permute-done.8
  83.3 3.0 collective-permute-start.10
  86.3 1.3 collective-permute-start.11
  87.8 4.1 %collective-permute-done.11 = bf16[1,34,256]{2,1,0:T(8,128)(2,1)S(1)} collective-permute-done((bf16[1,34,256]{2,1,0:T(8,128)(2,1)S(1)}, bf16[1,34,256]{2,1,0:T(8,128)(2,1)S(1)}, u32[]{:S(2)}, u32[]{:S(2)}) %collective-permute-start.11) | collective-permute-done | bytes 17440 | tf_op jit(solution)/shard_map/ppermute | solution.py:19
  92.4 0.9 convolution_select_fusion.3
  93.6 0.7 copy-done.1
  94.3 1.1 fusion.29
  97.7 2.6 collective-permute-start.13
  101.1 0.7 collective-permute-done.12
  101.8 1.9 collective-permute-start.14
  103.7 1.3 collective-permute-start.15
  105.3 4.1 %collective-permute-done.15 = bf16[1,34,256]{2,1,0:T(8,128)(2,1)S(1)} collective-permute-done((bf16[1,34,256]{2,1,0:T(8,128)(2,1)S(1)}, bf16[1,34,256]{2,1,0:T(8,128)(2,1)S(1)}, u32[]{:S(2)}, u32[]{:S(2)}) %collective-permute-start.15) | collective-permute-done | bytes 17440 | tf_op jit(solution)/shard_map/ppermute | solution.py:19
  109.8 1.0 convolution_select_fusion.2
  111.1 0.3 fusion.30
  111.4 0.4 fusion.31
  113.0 0.3 convolution_bitcast_fusion.9
  113.9 2.6 collective-permute-start.17
  117.3 0.6 collective-permute-done.16
  118.0 1.9 collective-permute-start.18
  119.9 1.3 collective-permute-start.19
  121.5 4.1 %collective-permute-done.19 = bf16[1,34,256]{2,1,0:T(8,128)(2,1)S(1)} collective-permute-done((bf16[1,34,256]{2,1,0:T(8,128)(2,1)S(1)}, bf16[1,34,256]{2,1,0:T(8,128)(2,1)S(1)}, u32[]{:S(2)}, u32[]{:S(2)}) %collective-permute-start.19) | collective-permute-done | bytes 17440 | tf_op jit(solution)/shard_map/ppermute | solution.py:19
  126.0 1.0 convolution_select_fusion.1
  127.3 0.3 fusion.32
  127.6 0.4 fusion.33
  129.8 2.6 collective-permute-start.21
  133.9 1.9 collective-permute-start.22
  135.8 1.5 collective-permute-start.23
  137.3 3.3 %pad_maximum_fusion = f32[3,3,3,256,256]{4,3,2,1,0:T(8,128)} fusion(f32[1,3,3,256,256]{4,3,2,1,0:T(8,128)S(1)} %maximum_multiply_fusion.2, f32[1,3,3,256,256]{4,3,2,1,0:T(8,128)S(1)} %maximum_multiply_fusion.1, f32[1,3,3,256,256]{4,3,2,1,0:T(8,128)S(1)} %maximum_multiply_fusion), kind=kLoop, calls=%fused_computation.11 | loop fusion | flops 3538944 | bytes 14155776 | tf_op jit(solution)/shard_map/stack | solution.py:140
  140.7 0.8 collective-permute-done.23
  141.9 1.0 convolution_select_fusion
  143.2 0.3 fusion.34
  143.5 0.3 convolution_multiply_fusion.1
  144.1 12.1 %gather_fusion = bf16[4096,128]{1,0:T(8,128)(2,1)S(1)} fusion(bf16[512,128]{1,0:T(8,128)(2,1)S(1)} %fusion.16, s32[4096]{0:T(1024)S(1)} %bitcast_clamp_fusion), kind=kCustom, calls=%fused_computation | custom fusion | bytes 2113536 | tf_op jit(solution)/shard_map/jit(_take)/gather | solution.py:143
  156.2 2.5 select_select_fusion
  158.7 3.7 %all-to-all-start.2 = ((bf16[32,128,128]{2,1,0:T(8,128)(2,1)}), bf16[32,128,128]{2,1,0:T(8,128)(2,1)S(1)}, u32[]{:S(2)}, u32[]{:S(2)}) async-start(bf16[32,128,128]{2,1,0:T(8,128)(2,1)} %select_select_fusion), calls=%async_computation.2 | async-start | bytes 2097152 | tf_op jit(solution)/shard_map/all_to_all | solution.py:145
  162.3 143.6 %all-reduce.2 = (bf16[3,3,3,256,256]{4,3,2,1,0:T(8,128)(2,1)}, bf16[128,256]{1,0:T(8,128)(2,1)}) all-reduce(f32[3,3,3,256,256]{4,3,2,1,0:T(8,128)} %pad_maximum_fusion, f32[128,256]{1,0:T(8,128)S(1)} %convolution_multiply_fusion.1), channel_id=1, replica_groups=mesh['lon'=8,'lat'=4] {'lon','lat'}, use_global_device_ids=true, to_apply=%region_3.4 | all-reduce | flops 1802240 | bytes 10813440 | tf_op jit(solution)/shard_map/psum | solution.py:140
  305.9 1.0 copy.187
  (128 shorter events, 14.4 us)
Async XLA Ops:
  0.6 47.3 %copy-start = (bf16[128,256]{1,0:T(8,128)(2,1)S(1)}, bf16[128,256]{1,0:T(8,128)(2,1)}, u32[]{:S(2)}) copy-start(bf16[128,256]{1,0:T(8,128)(2,1)} %param.12) | copy-start | bytes 196612
  15.7 27.7 %all-to-all-start.1 = ((bf16[32,128,128]{2,1,0:T(8,128)(2,1)}), bf16[32,128,128]{2,1,0:T(8,128)(2,1)S(1)}, u32[]{:S(2)}, u32[]{:S(2)}) async-start(bf16[32,128,128]{2,1,0:T(8,128)(2,1)} %bitcast.265), calls=%async_computation.1 | async-start | bytes 2097152 | tf_op jit(solution)/shard_map/all_to_all | solution.py:52
  47.9 15.8 %copy-start.2 = (bf16[3,3,3,256,256]{4,3,2,1,0:T(8,128)(2,1)S(1)}, bf16[3,3,3,256,256]{4,3,2,1,0:T(8,128)(2,1)}, u32[]{:S(2)}) copy-start(bf16[3,3,3,256,256]{4,3,2,1,0:T(8,128)(2,1)} %param.14) | copy-start | bytes 10616836
  47.9 15.8 %copy-start.3 = (pred[8,5]{0,1:T(8,128)(4,1)S(1)}, pred[8,5]{0,1:T(8,128)(4,1)}, u32[]{:S(2)}) copy-start(pred[8,5]{0,1:T(8,128)(4,1)} %constant.95) | copy-start | bytes 124
  48.2 4.1 %collective-permute-start = (bf16[16,1,256]{2,1,0:T(2,128)(2,1)S(1)}, bf16[16,1,256]{2,1,0:T(2,128)(2,1)S(1)}, u32[]{:S(2)}, u32[]{:S(2)}) collective-permute-start(bf16[16,1,256]{2,1,0:T(2,128)(2,1)S(1)} %get-tuple-element.178), channel_id=1, source_target_pairs={{0,4},{4,8},{8,12},{12,16},{16,20},{20,24},{24,28},{28,0},{1,5},{5... | collective-permute-start | bytes 24584 | tf_op jit(solution)/shard_map/ppermute | solution.py:16
  49.9 2.6 collective-permute-start.1
  52.4 6.6 %collective-permute-start.2 = (bf16[1,34,256]{2,1,0:T(8,128)(2,1)S(1)}, bf16[1,34,256]{2,1,0:T(8,128)(2,1)S(1)}, u32[]{:S(2)}, u32[]{:S(2)}) collective-permute-start(bf16[1,34,256]{2,1,0:T(8,128)(2,1)S(1)} %get-tuple-element.166), channel_id=1, source_target_pairs={{0,1},{1,2},{2,3},{4,5},{5,6},{6,7},{8,9},{9,10},{10,11},{12,13},{... | collective-permute-start | bytes 52232 | tf_op jit(solution)/shard_map/ppermute | solution.py:16
  57.5 5.7 %collective-permute-start.3 = (bf16[1,34,256]{2,1,0:T(8,128)(2,1)S(1)}, bf16[1,34,256]{2,1,0:T(8,128)(2,1)S(1)}, u32[]{:S(2)}, u32[]{:S(2)}) collective-permute-start(bf16[1,34,256]{2,1,0:T(8,128)(2,1)S(1)} %get-tuple-element.167), channel_id=1, source_target_pairs={{1,0},{2,1},{3,2},{5,4},{6,5},{7,6},{9,8},{10,9},{11,10},{13,12},{... | collective-permute-start | bytes 52232 | tf_op jit(solution)/shard_map/ppermute | solution.py:19
  65.3 4.1 %collective-permute-start.4 = (bf16[16,1,256]{2,1,0:T(2,128)(2,1)S(1)}, bf16[16,1,256]{2,1,0:T(2,128)(2,1)S(1)}, u32[]{:S(2)}, u32[]{:S(2)}) collective-permute-start(bf16[16,1,256]{2,1,0:T(2,128)(2,1)S(1)} %get-tuple-element.176), channel_id=1, source_target_pairs={{0,4},{4,8},{8,12},{12,16},{16,20},{20,24},{24,28},{28,0},{1,5},{5... | collective-permute-start | bytes 24584 | tf_op jit(solution)/shard_map/ppermute | solution.py:16
  65.4 4.1 %collective-permute-start.5 = (bf16[16,1,256]{2,1,0:T(2,128)(2,1)S(1)}, bf16[16,1,256]{2,1,0:T(2,128)(2,1)S(1)}, u32[]{:S(2)}, u32[]{:S(2)}) collective-permute-start(bf16[16,1,256]{2,1,0:T(2,128)(2,1)S(1)} %get-tuple-element.177), channel_id=1, source_target_pairs={{4,0},{8,4},{12,8},{16,12},{20,16},{24,20},{28,24},{0,28},{5,1},{9... | collective-permute-start | bytes 24584 | tf_op jit(solution)/shard_map/ppermute | solution.py:19
  69.5 3.4 %collective-permute-start.6 = (bf16[1,34,256]{2,1,0:T(8,128)(2,1)S(1)}, bf16[1,34,256]{2,1,0:T(8,128)(2,1)S(1)}, u32[]{:S(2)}, u32[]{:S(2)}) collective-permute-start(bf16[1,34,256]{2,1,0:T(8,128)(2,1)S(1)} %get-tuple-element.164), channel_id=1, source_target_pairs={{0,1},{1,2},{2,3},{4,5},{5,6},{6,7},{8,9},{9,10},{10,11},{12,13},{... | collective-permute-start | bytes 52232 | tf_op jit(solution)/shard_map/ppermute | solution.py:16
  71.4 5.7 %collective-permute-start.7 = (bf16[1,34,256]{2,1,0:T(8,128)(2,1)S(1)}, bf16[1,34,256]{2,1,0:T(8,128)(2,1)S(1)}, u32[]{:S(2)}, u32[]{:S(2)}) collective-permute-start(bf16[1,34,256]{2,1,0:T(8,128)(2,1)S(1)} %get-tuple-element.165), channel_id=1, source_target_pairs={{1,0},{2,1},{3,2},{5,4},{6,5},{7,6},{9,8},{10,9},{11,10},{13,12},{... | collective-permute-start | bytes 52232 | tf_op jit(solution)/shard_map/ppermute | solution.py:19
  79.1 4.1 %collective-permute-start.8 = (bf16[16,1,256]{2,1,0:T(2,128)(2,1)S(1)}, bf16[16,1,256]{2,1,0:T(2,128)(2,1)S(1)}, u32[]{:S(2)}, u32[]{:S(2)}) collective-permute-start(bf16[16,1,256]{2,1,0:T(2,128)(2,1)S(1)} %get-tuple-element.174), channel_id=1, source_target_pairs={{0,4},{4,8},{8,12},{12,16},{16,20},{20,24},{24,28},{28,0},{1,5},{5... | collective-permute-start | bytes 24584 | tf_op jit(solution)/shard_map/ppermute | solution.py:16
  79.2 4.1 %collective-permute-start.9 = (bf16[16,1,256]{2,1,0:T(2,128)(2,1)S(1)}, bf16[16,1,256]{2,1,0:T(2,128)(2,1)S(1)}, u32[]{:S(2)}, u32[]{:S(2)}) collective-permute-start(bf16[16,1,256]{2,1,0:T(2,128)(2,1)S(1)} %get-tuple-element.175), channel_id=1, source_target_pairs={{4,0},{8,4},{12,8},{16,12},{20,16},{24,20},{28,24},{0,28},{5,1},{9... | collective-permute-start | bytes 24584 | tf_op jit(solution)/shard_map/ppermute | solution.py:19
  83.3 4.5 %collective-permute-start.10 = (bf16[1,34,256]{2,1,0:T(8,128)(2,1)S(1)}, bf16[1,34,256]{2,1,0:T(8,128)(2,1)S(1)}, u32[]{:S(2)}, u32[]{:S(2)}) collective-permute-start(bf16[1,34,256]{2,1,0:T(8,128)(2,1)S(1)} %get-tuple-element.162), channel_id=1, source_target_pairs={{0,1},{1,2},{2,3},{4,5},{5,6},{6,7},{8,9},{9,10},{10,11},{12,13},{... | collective-permute-start | bytes 52232 | tf_op jit(solution)/shard_map/ppermute | solution.py:16
  86.3 5.7 %collective-permute-start.11 = (bf16[1,34,256]{2,1,0:T(8,128)(2,1)S(1)}, bf16[1,34,256]{2,1,0:T(8,128)(2,1)S(1)}, u32[]{:S(2)}, u32[]{:S(2)}) collective-permute-start(bf16[1,34,256]{2,1,0:T(8,128)(2,1)S(1)} %get-tuple-element.163), channel_id=1, source_target_pairs={{1,0},{2,1},{3,2},{5,4},{6,5},{7,6},{9,8},{10,9},{11,10},{13,12},{... | collective-permute-start | bytes 52232 | tf_op jit(solution)/shard_map/ppermute | solution.py:19
  93.4 1.0 copy-start.1
  97.6 4.1 %collective-permute-start.12 = (bf16[16,1,256]{2,1,0:T(2,128)(2,1)S(1)}, bf16[16,1,256]{2,1,0:T(2,128)(2,1)S(1)}, u32[]{:S(2)}, u32[]{:S(2)}) collective-permute-start(bf16[16,1,256]{2,1,0:T(2,128)(2,1)S(1)} %get-tuple-element.172), channel_id=1, source_target_pairs={{0,4},{4,8},{8,12},{12,16},{16,20},{20,24},{24,28},{28,0},{1,5},{5... | collective-permute-start | bytes 24584 | tf_op jit(solution)/shard_map/ppermute | solution.py:16
  97.7 4.1 %collective-permute-start.13 = (bf16[16,1,256]{2,1,0:T(2,128)(2,1)S(1)}, bf16[16,1,256]{2,1,0:T(2,128)(2,1)S(1)}, u32[]{:S(2)}, u32[]{:S(2)}) collective-permute-start(bf16[16,1,256]{2,1,0:T(2,128)(2,1)S(1)} %get-tuple-element.173), channel_id=1, source_target_pairs={{4,0},{8,4},{12,8},{16,12},{20,16},{24,20},{28,24},{0,28},{5,1},{9... | collective-permute-start | bytes 24584 | tf_op jit(solution)/shard_map/ppermute | solution.py:19
  101.8 3.5 %collective-permute-start.14 = (bf16[1,34,256]{2,1,0:T(8,128)(2,1)S(1)}, bf16[1,34,256]{2,1,0:T(8,128)(2,1)S(1)}, u32[]{:S(2)}, u32[]{:S(2)}) collective-permute-start(bf16[1,34,256]{2,1,0:T(8,128)(2,1)S(1)} %get-tuple-element.158), channel_id=1, source_target_pairs={{0,1},{1,2},{2,3},{4,5},{5,6},{6,7},{8,9},{9,10},{10,11},{12,13},{... | collective-permute-start | bytes 52232 | tf_op jit(solution)/shard_map/ppermute | solution.py:16
  103.7 5.7 %collective-permute-start.15 = (bf16[1,34,256]{2,1,0:T(8,128)(2,1)S(1)}, bf16[1,34,256]{2,1,0:T(8,128)(2,1)S(1)}, u32[]{:S(2)}, u32[]{:S(2)}) collective-permute-start(bf16[1,34,256]{2,1,0:T(8,128)(2,1)S(1)} %get-tuple-element.159), channel_id=1, source_target_pairs={{1,0},{2,1},{3,2},{5,4},{6,5},{7,6},{9,8},{10,9},{11,10},{13,12},{... | collective-permute-start | bytes 52232 | tf_op jit(solution)/shard_map/ppermute | solution.py:19
  113.8 4.1 %collective-permute-start.16 = (bf16[16,1,256]{2,1,0:T(2,128)(2,1)S(1)}, bf16[16,1,256]{2,1,0:T(2,128)(2,1)S(1)}, u32[]{:S(2)}, u32[]{:S(2)}) collective-permute-start(bf16[16,1,256]{2,1,0:T(2,128)(2,1)S(1)} %get-tuple-element.170), channel_id=1, source_target_pairs={{0,4},{4,8},{8,12},{12,16},{16,20},{20,24},{24,28},{28,0},{1,5},{5... | collective-permute-start | bytes 24584 | tf_op jit(solution)/shard_map/ppermute | solution.py:16
  113.9 4.1 %collective-permute-start.17 = (bf16[16,1,256]{2,1,0:T(2,128)(2,1)S(1)}, bf16[16,1,256]{2,1,0:T(2,128)(2,1)S(1)}, u32[]{:S(2)}, u32[]{:S(2)}) collective-permute-start(bf16[16,1,256]{2,1,0:T(2,128)(2,1)S(1)} %get-tuple-element.171), channel_id=1, source_target_pairs={{4,0},{8,4},{12,8},{16,12},{20,16},{24,20},{28,24},{0,28},{5,1},{9... | collective-permute-start | bytes 24584 | tf_op jit(solution)/shard_map/ppermute | solution.py:19
  118.0 3.5 %collective-permute-start.18 = (bf16[1,34,256]{2,1,0:T(8,128)(2,1)S(1)}, bf16[1,34,256]{2,1,0:T(8,128)(2,1)S(1)}, u32[]{:S(2)}, u32[]{:S(2)}) collective-permute-start(bf16[1,34,256]{2,1,0:T(8,128)(2,1)S(1)} %get-tuple-element.154), channel_id=1, source_target_pairs={{0,1},{1,2},{2,3},{4,5},{5,6},{6,7},{8,9},{9,10},{10,11},{12,13},{... | collective-permute-start | bytes 52232 | tf_op jit(solution)/shard_map/ppermute | solution.py:16
  119.9 5.7 %collective-permute-start.19 = (bf16[1,34,256]{2,1,0:T(8,128)(2,1)S(1)}, bf16[1,34,256]{2,1,0:T(8,128)(2,1)S(1)}, u32[]{:S(2)}, u32[]{:S(2)}) collective-permute-start(bf16[1,34,256]{2,1,0:T(8,128)(2,1)S(1)} %get-tuple-element.155), channel_id=1, source_target_pairs={{1,0},{2,1},{3,2},{5,4},{6,5},{7,6},{9,8},{10,9},{11,10},{13,12},{... | collective-permute-start | bytes 52232 | tf_op jit(solution)/shard_map/ppermute | solution.py:19
  129.7 4.1 %collective-permute-start.20 = (bf16[16,1,256]{2,1,0:T(2,128)(2,1)S(1)}, bf16[16,1,256]{2,1,0:T(2,128)(2,1)S(1)}, u32[]{:S(2)}, u32[]{:S(2)}) collective-permute-start(bf16[16,1,256]{2,1,0:T(2,128)(2,1)S(1)} %get-tuple-element.168), channel_id=1, source_target_pairs={{0,4},{4,8},{8,12},{12,16},{16,20},{20,24},{24,28},{28,0},{1,5},{5... | collective-permute-start | bytes 24584 | tf_op jit(solution)/shard_map/ppermute | solution.py:16
  129.8 4.1 %collective-permute-start.21 = (bf16[16,1,256]{2,1,0:T(2,128)(2,1)S(1)}, bf16[16,1,256]{2,1,0:T(2,128)(2,1)S(1)}, u32[]{:S(2)}, u32[]{:S(2)}) collective-permute-start(bf16[16,1,256]{2,1,0:T(2,128)(2,1)S(1)} %get-tuple-element.169), channel_id=1, source_target_pairs={{4,0},{8,4},{12,8},{16,12},{20,16},{24,20},{28,24},{0,28},{5,1},{9... | collective-permute-start | bytes 24584 | tf_op jit(solution)/shard_map/ppermute | solution.py:19
  133.9 6.8 %collective-permute-start.22 = (bf16[1,34,256]{2,1,0:T(8,128)(2,1)S(1)}, bf16[1,34,256]{2,1,0:T(8,128)(2,1)S(1)}, u32[]{:S(2)}, u32[]{:S(2)}) collective-permute-start(bf16[1,34,256]{2,1,0:T(8,128)(2,1)S(1)} %get-tuple-element.150), channel_id=1, source_target_pairs={{0,1},{1,2},{2,3},{4,5},{5,6},{6,7},{8,9},{9,10},{10,11},{12,13},{... | collective-permute-start | bytes 52232 | tf_op jit(solution)/shard_map/ppermute | solution.py:16
  135.8 5.7 %collective-permute-start.23 = (bf16[1,34,256]{2,1,0:T(8,128)(2,1)S(1)}, bf16[1,34,256]{2,1,0:T(8,128)(2,1)S(1)}, u32[]{:S(2)}, u32[]{:S(2)}) collective-permute-start(bf16[1,34,256]{2,1,0:T(8,128)(2,1)S(1)} %get-tuple-element.151), channel_id=1, source_target_pairs={{1,0},{2,1},{3,2},{5,4},{6,5},{7,6},{9,8},{10,9},{11,10},{13,12},{... | collective-permute-start | bytes 52232 | tf_op jit(solution)/shard_map/ppermute | solution.py:19
  158.7 147.2 %all-to-all-start.2 = ((bf16[32,128,128]{2,1,0:T(8,128)(2,1)}), bf16[32,128,128]{2,1,0:T(8,128)(2,1)S(1)}, u32[]{:S(2)}, u32[]{:S(2)}) async-start(bf16[32,128,128]{2,1,0:T(8,128)(2,1)} %select_select_fusion), calls=%async_computation.2 | async-start | bytes 2097152 | tf_op jit(solution)/shard_map/all_to_all | solution.py:145
where the time goes:
time: 308 us; the launch traced here: 307 us
  blocking collectives  158 us (51%)
  waiting for transfers between devices  52 us (17%)
  starting transfers between devices  46.3 us (15%)
  matrix products  17.1 us (6%)
  local copies, waits for them, and re-layouts  16.8 us (5%)
  other arithmetic  15.2 us (5%)
    psum x1, blocking collectives, on_device(): lax.psum((jnp.stack(kernel_grads), embed_grad), ('lon', 'lat'))  144 us
    all_to_all x1, waiting for transfers between devices, on_device(): lax.all_to_all(obs_rows, ('lon', 'lat'), split_axis=0, concat_axis=0, til...  24.4 us
    ppermute x12, starting transfers between devices, extended(): lax.ppermute(lax.slice_in_dim(block, 0, width, axis=dim), axis, backward)  22.2 us
    ppermute x12, waiting for transfers between devices, extended(): lax.ppermute(lax.slice_in_dim(block, 0, width, axis=dim), axis, backward)  21.9 us
    ppermute x12, starting transfers between devices, extended(): lax.ppermute(lax.slice_in_dim(block, block.shape[dim] - width, None, axis...  17.7 us
    all_to_all x1, blocking collectives, on_device(): lax.all_to_all(sent_ids, ('lon', 'lat'), split_axis=0, concat_axis=0, til...  14.3 us
    gather x1, local copies, waits for them, and re-layouts, on_device(): picked = jnp.take(cell_grad, jnp.maximum(got_ids, 0), axis=0)  12.1 us
    dot_general x27, matrix products, on_device(): lax.dot_general(window, slope_flat, (((0,), (0,)), ((), ())), preferred_e...  7.3 us
  transfers between devices with their start and end apart: 26, of which 16 were waited for; matrix products, arithmetic and copies ran while one was open for 2% of the time, Pallas kernels for 0%

commit v1 on v0

v1 whole, which is shorter than its diff:
```python
import math

import jax
import jax.numpy as jnp
from jax import lax
from jax.sharding import PartitionSpec as P

ID_BASE = 128


def shift_pairs(count, step, periodic):
    pairs = []
    for source in range(count):
        target = source + step
        if 0 <= target < count:
            pairs.append((source, target))
        elif periodic:
            pairs.append((source, target % count))
    return pairs


def widen(block, depth):
    lon_count = lax.axis_size("lon")
    lat_count = lax.axis_size("lat")
    west = lax.ppermute(block[:, -depth:], "lon", shift_pairs(lon_count, 1, True))
    east = lax.ppermute(block[:, :depth], "lon", shift_pairs(lon_count, -1, True))
    block = jnp.concatenate([west, block, east], axis=1)
    north = lax.ppermute(block[-depth:], "lat", shift_pairs(lat_count, 1, False))
    south = lax.ppermute(block[:depth], "lat", shift_pairs(lat_count, -1, False))
    return jnp.concatenate([north, block, south], axis=0)


def lat_mask(rows, margin, height):
    lat_index = lax.axis_index("lat")
    lat_count = lax.axis_size("lat")
    global_row = lat_index * height - margin + jnp.arange(rows, dtype=jnp.int32)
    return ((global_row >= 0) & (global_row < lat_count * height))[:, None, None]


def crop(field, margin):
    if margin == 0:
        return field
    return field[margin:-margin, margin:-margin]


def conv_valid(padded, kernel):
    return lax.conv_general_dilated(
        padded[None],
        kernel,
        (1, 1),
        "VALID",
        dimension_numbers=("NHWC", "HWIO", "NHWC"),
        preferred_element_type=jnp.float32,
    )[0]


def reduce_replicated(parts):
    flat = jnp.concatenate([part.reshape(-1) for part in parts])
    summed = lax.psum_scatter(flat, ("lon", "lat"), scatter_dimension=0, tiled=True)
    return summed


def on_device(obs_rows, cell_ids, counts, w_embed, w_density, kernels, cotangent):
    lon_count = lax.axis_size("lon")
    lat_count = lax.axis_size("lat")
    devices = lon_count * lat_count
    height, tile_width, channels = cotangent.shape
    cell_count = height * tile_width
    slot_rows = obs_rows.shape[0] // devices
    feat_count = obs_rows.shape[1]
    layer_count = kernels.shape[0]
    margin = 2 * layer_count

    cot_wide = widen(cotangent, layer_count)

    live_mask = jnp.arange(slot_rows, dtype=jnp.int32)[None, :] < counts[0][:, None]
    slot_ids = cell_ids.reshape(devices, slot_rows)
    id_high = jnp.where(live_mask, slot_ids // ID_BASE, -1)
    id_low = jnp.where(live_mask, slot_ids % ID_BASE, -1)
    code = jnp.concatenate([id_high, id_low], axis=1).astype(jnp.bfloat16)
    code_rows = -(-2 * slot_rows // feat_count)
    code_pad = -(-code_rows // 16) * 16
    code = jnp.pad(code, ((0, 0), (0, code_rows * feat_count - 2 * slot_rows)))
    code = code.reshape(devices, code_rows, feat_count)
    code = jnp.pad(code, ((0, 0), (0, code_pad - code_rows), (0, 0)))
    packed = jnp.concatenate([obs_rows.reshape(devices, slot_rows, feat_count), code], axis=1)
    got = lax.all_to_all(packed, ("lon", "lat"), split_axis=0, concat_axis=0, tiled=True)
    got_rows = got[:, :slot_rows].reshape(devices * slot_rows, feat_count)
    got_code = got[:, slot_rows : slot_rows + code_rows].reshape(devices, code_rows * feat_count)
    got_code = got_code.astype(jnp.int32)
    got_ids = (got_code[:, :slot_rows] * ID_BASE + got_code[:, slot_rows : 2 * slot_rows]).reshape(-1)

    cell_iota = jnp.arange(cell_count, dtype=jnp.int32)
    onehot = (got_ids[:, None] == cell_iota[None, :]).astype(jnp.bfloat16)
    cell_sums = lax.dot_general(
        onehot, got_rows, (((0,), (0,)), ((), ())), preferred_element_type=jnp.float32
    )
    density = jnp.sum(onehot.astype(jnp.float32), axis=0)
    inv_root = lax.rsqrt(density + 1.0)
    features = (cell_sums * inv_root[:, None]).astype(jnp.bfloat16)
    start_act = (
        jnp.dot(features, w_embed, preferred_element_type=jnp.float32)
        + jnp.log1p(density)[:, None] * w_density.astype(jnp.float32)[None, :]
    )
    activation = start_act.astype(jnp.bfloat16).reshape(height, tile_width, channels)

    act = widen(activation, margin)
    stored_acts = [act]
    stored_pre = []
    for layer_index in range(layer_count):
        out_margin = margin - layer_index - 1
        preact = conv_valid(act, kernels[layer_index])
        act = (crop(act, 1).astype(jnp.float32) + jax.nn.silu(preact)).astype(jnp.bfloat16)
        act = jnp.where(lat_mask(act.shape[0], out_margin, height), act, jnp.zeros_like(act))
        stored_pre.append(preact)
        stored_acts.append(act)
    encoded = crop(act, margin - layer_count)

    grad_scale = 1.0 / math.sqrt(cell_count * devices)
    back = cot_wide
    reduced = [None] * layer_count
    for layer_index in reversed(range(layer_count)):
        back_margin = layer_index + 1
        preact = crop(stored_pre[layer_index], margin - layer_index - 1 - back_margin)
        sigmoid_v = jax.nn.sigmoid(preact)
        slope = (
            back.astype(jnp.float32) * (sigmoid_v * (1.0 + preact * (1.0 - sigmoid_v)))
        ).astype(jnp.bfloat16)
        slope = jnp.where(lat_mask(slope.shape[0], back_margin, height), slope, jnp.zeros_like(slope))
        slope_flat = crop(slope, back_margin).reshape(cell_count, channels)
        act_in = crop(stored_acts[layer_index], margin - layer_index - 1)
        tap_rows = []
        for row_off in range(3):
            tap_cols = []
            for col_off in range(3):
                window = act_in[row_off : row_off + height, col_off : col_off + tile_width].reshape(
                    cell_count, channels
                )
                tap_cols.append(
                    lax.dot_general(
                        window,
                        slope_flat,
                        (((0,), (0,)), ((), ())),
                        preferred_element_type=jnp.float32,
                    )
                )
            tap_rows.append(jnp.stack(tap_cols))
        tap_grad = jnp.stack(tap_rows)
        flipped = jnp.transpose(kernels[layer_index][::-1, ::-1], (0, 1, 3, 2))
        spread = conv_valid(slope, flipped)
        back = lax.optimization_barrier(
            (crop(back, 1).astype(jnp.float32) + spread).astype(jnp.bfloat16)
        )
        if layer_index > 0:
            reduced[layer_index] = reduce_replicated([tap_grad])
        else:
            last_grad = tap_grad
    back_flat = back.reshape(cell_count, channels)
    embed_grad = lax.dot_general(
        features, back_flat, (((0,), (0,)), ((), ())), preferred_element_type=jnp.float32
    )
    reduced[0] = reduce_replicated([last_grad, embed_grad])
    cell_grad = (
        lax.dot_general(
            back_flat, w_embed, (((1,), (1,)), ((), ())), preferred_element_type=jnp.float32
        )
        * inv_root[:, None]
    ).astype(jnp.bfloat16)
    picked = jnp.dot(onehot, cell_grad, preferred_element_type=jnp.float32).astype(jnp.bfloat16)
    grad_obs = lax.all_to_all(picked, ("lon", "lat"), split_axis=0, concat_axis=0, tiled=True)

    tap_size = kernels[0].size
    gathered = [
        lax.all_gather((part * grad_scale).astype(jnp.bfloat16), ("lon", "lat"), axis=0, tiled=True)
        for part in reduced
    ]
    kernel_out = jnp.stack(
        [gathered[0][:tap_size]] + [gathered[index] for index in range(1, layer_count)]
    ).reshape(kernels.shape)
    embed_out = gathered[0][tap_size:].reshape(w_embed.shape)
    return (encoded, kernel_out, embed_out, grad_obs)


def solution(mesh):
    placed = (
        P(("lon", "lat"), None),
        P(("lon", "lat")),
        P(("lon", "lat"), None),
        P(),
        P(),
        P(),
        P("lat", "lon", None),
    )
    return jax.shard_map(
        on_device,
        mesh=mesh,
        in_specs=placed,
        out_specs=(P("lat", "lon", None), P(), P(), P(("lon", "lat"), None)),
        check_vma=False,
    )
```

time: 308 us -> 483 us (1.57); the launches traced: 307 us -> 475 us
  waiting for transfers between devices: 52 us -> 325 us
  blocking collectives: 158 us -> 30.8 us
  starting transfers between devices: 46.3 us -> 24.4 us
  local copies, waits for them, and re-layouts: 16.8 us -> 31.5 us
  between operations: 1.63 us -> 15.3 us
  other arithmetic: 15.2 us -> 24.4 us
  matrix products: 17.1 us -> 23.8 us
    unnamed x0 -> x5, waiting for transfers between devices: none -> 166 us
    psum x1 -> x0, blocking collectives: 144 us -> none  [on_device(): lax.psum((jnp.stack(kernel_grads), embed_grad), ('lon', 'lat'))]
    all_gather x0 -> x3, waiting for transfers between devices: none -> 133 us  [on_device(): lax.all_gather((part * grad_scale).astype(jnp.bfloat16), ('lon', 'lat'),...]
    ppermute x24 -> x8, starting transfers between devices: 39.9 us -> 16.9 us  [the longest x2 9.14 us: widen(): lax.ppermute(block[-depth:], 'lat', shift_pairs(lat_count, 1, False))]
    ppermute x24 -> x8, waiting for transfers between devices: 27.6 us -> 8.77 us  [the longest x2 4.44 us: widen(): lax.ppermute(block[:, :depth], 'lon', shift_pairs(lon_count, -1, True))]
    all_to_all x1, blocking collectives: 14.3 us -> 30.8 us  [on_device(): lax.all_to_all(picked, ('lon', 'lat'), split_axis=0, concat_axis=0, tiled...]
    gather x1 -> x0, local copies, waits for them, and re-layouts: 12.1 us -> none  [on_device(): picked = jnp.take(cell_grad, jnp.maximum(got_ids, 0), axis=0)]
    unnamed x15 -> x63, local copies, waits for them, and re-layouts: 2.11 us -> 13.4 us
  transfers between devices with their start and end apart: 26 -> 13, of which waited for: 16 -> 9; matrix products, arithmetic and copies ran while one was open for 2% -> 3% of each run, Pallas kernels for 0% -> 0%
where the time goes in v1:
time: 483 us; the launch traced here: 475 us
  waiting for transfers between devices  325 us (67%)
  local copies, waits for them, and re-layouts  31.5 us (7%)
  blocking collectives  30.8 us (6%)
  other arithmetic  24.4 us (5%)
  starting transfers between devices  24.4 us (5%)
  matrix products  23.8 us (5%)
  between operations  15.3 us (3%)
    unnamed x5, waiting for transfers between devices  166 us
    all_gather x3, waiting for transfers between devices, on_device(): lax.all_gather((part * grad_scale).astype(jnp.bfloat16), ('lon', 'lat'),...  133 us
    all_to_all x1, blocking collectives, on_device(): lax.all_to_all(picked, ('lon', 'lat'), split_axis=0, concat_axis=0, tiled...  30.8 us
    all_to_all x1, waiting for transfers between devices, on_device(): lax.all_to_all(packed, ('lon', 'lat'), split_axis=0, concat_axis=0, tiled...  16.5 us
    unnamed x63, local copies, waits for them, and re-layouts  13.4 us
    conv_general_dilated x6, matrix products, conv_valid(): lax.conv_general_dilated(padded[None], kernel, (1, 1), 'VALID', dimension...  10.2 us
  transfers between devices with their start and end apart: 13, of which 9 were waited for; matrix products, arithmetic and copies ran while one was open for 3% of the time, Pallas kernels for 0%

profile of v1, /device:TPU:0, one launch (start us, length us, event | category | flops | bytes accessed | tf_op | source)
XLA Modules:
  0.0 475.3 jit_solution(3114485129641464012)
XLA Ops:
  7.2 0.9 fusion.119
  8.0 0.8 fusion.120
  8.9 2.3 pad_maximum_fusion.5
  11.2 7.3 %all-to-all-start = ((bf16[32,144,128]{2,1,0:T(8,128)(2,1)}), bf16[32,144,128]{2,1,0:T(8,128)(2,1)S(1)}, u32[]{:S(2)}, u32[]{:S(2)}) async-start(bf16[32,144,128]{2,1,0:T(8,128)(2,1)} %pad_maximum_fusion.5), calls=%async_computation | async-start | bytes 2359296 | tf_op jit(solution)/shard_map/all_to_all | solution.py:87
  18.6 2.5 collective-permute-start.5
  21.1 0.5 compare_and_fusion.2
  21.7 4.4 collective-permute-done.5
  26.1 2.8 collective-permute-done.4
  28.9 0.9 fusion.160
  29.8 16.5 %all-to-all-done = bf16[32,144,128]{2,1,0:T(8,128)(2,1)S(1)} async-done(((bf16[32,144,128]{2,1,0:T(8,128)(2,1)}), bf16[32,144,128]{2,1,0:T(8,128)(2,1)S(1)}, u32[]{:S(2)}, u32[]{:S(2)}) %all-to-all-start) | async-done | bytes 1179680 | tf_op jit(solution)/shard_map/all_to_all | solution.py:87
  46.3 1.0 convert_reduce_fusion
  47.5 3.0 fusion.19
  50.7 2.7 collective-permute-start.1
  53.4 1.3 collective-permute-start.7
  54.7 4.6 collective-permute-start.6
  59.5 1.3 collective-permute-start.3
  60.8 4.6 collective-permute-start.2
  65.3 0.6 slice.307
  65.9 0.9 pad_maximum_fusion.8
  67.2 1.2 collective-permute-done.2
  69.7 2.9 convolution_select_fusion
  72.6 0.5 copy.77
  73.3 1.1 pad_maximum_fusion.6
  74.5 0.5 broadcast_select_fusion
  75.0 0.9 pad.7
  75.9 1.5 reshape.308
  77.6 2.8 convolution_select_fusion.1
  80.4 0.7 copy.80
  81.2 0.6 broadcast_select_fusion.1
  82.2 1.0 copy-done.18
  83.2 1.3 add_multiply_fusion
  84.9 0.4 broadcast_subtract_fusion
  85.5 0.7 copy-done.1
  86.3 1.2 fusion.84
  90.8 0.9 copy-done.5
  92.7 1.2 convolution_select_fusion.3
  94.5 0.4 broadcast_select_fusion.2
  95.2 0.5 convolution_bitcast_fusion.10
  98.5 0.4 copy-done.21
  98.9 1.1 convolution_select_fusion.4
  104.0 2.6 copy.118
  106.9 2.7 copy.117
  109.8 0.4 copy-done.20
  110.3 1.0 convolution_select_fusion.5
  111.9 0.5 copy-done.9
  113.5 0.4 pad_maximum_fusion.2
  113.9 1.2 copy.115
  115.2 1.6 pad_maximum_fusion.1
  116.8 166.4 %all-reduce.7.cloned.1.call-done = (f32[589824]{0:T(1024)}, f32[589824]{0:T(1024)}, f32[622592]{0:T(1024)}) async-done(((f32[589824]{0:T(1024)}, f32[589824]{0:T(1024)}, f32[622592]{0:T(1024)}), (f32[589824]{0:T(1024)}, f32[589824]{0:T(1024)}, f32[622592]{0:T(1024)})) %all-reduce.7.cloned.1.call-update) | async-done | bytes 7208976
  283.2 1.5 fusion.117
  284.8 1.5 fusion.118
  286.4 1.5 fusion.116
  287.9 1.7 fusion.3
  289.7 30.8 %all_to_all.17 = bf16[32,128,128]{2,1,0:T(8,128)(2,1)S(1)} all-to-all(bf16[32,128,128]{2,1,0:T(8,128)(2,1)S(1)} %bitcast.273), channel_id=1, replica_groups=mesh['lon'=8,'lat'=4] {'lon','lat'}, dimensions={0} | all-to-all | bytes 2097152 | tf_op jit(solution)/shard_map/all_to_all | solution.py:170
  320.5 24.0 %all-gather.8.cloned.1.call-done = bf16[589824]{0:T(1024)(128)(2,1)} async-done(((bf16[18432]{0:T(1024)(128)(2,1)}), bf16[589824]{0:T(1024)(128)(2,1)}) %all-gather.8.cloned.1.call-update) | async-done | bytes 1179664 | tf_op jit(solution)/shard_map/all_gather | solution.py:174
  344.6 2.2 stack.206
  346.8 54.6 %all-gather.6.cloned.1.call-done = bf16[589824]{0:T(1024)(128)(2,1)} async-done(((bf16[18432]{0:T(1024)(128)(2,1)}), bf16[589824]{0:T(1024)(128)(2,1)}) %all-gather.6.cloned.1.call-update) | async-done | bytes 1179664 | tf_op jit(solution)/shard_map/all_gather | solution.py:174
  401.4 2.2 stack.189
  403.6 54.7 %all-gather.4.cloned.1.call-done = bf16[622592]{0:T(1024)(128)(2,1)} async-done(((bf16[19456]{0:T(1024)(128)(2,1)}), bf16[622592]{0:T(1024)(128)(2,1)}) %all-gather.4.cloned.1.call-update) | async-done | bytes 1245200 | tf_op jit(solution)/shard_map/all_gather | solution.py:174
  458.3 2.4 slice.329
  460.7 3.0 stack.172
  463.7 0.7 slice.275
  464.4 3.0 pad_maximum_fusion
  467.4 1.0 copy.155
  (159 shorter events, 17.8 us)
Async XLA Ops:
  7.2 43.3 %copy-start = (bf16[128,256]{1,0:T(8,128)(2,1)S(1)}, bf16[128,256]{1,0:T(8,128)(2,1)}, u32[]{:S(2)}) copy-start(bf16[128,256]{1,0:T(8,128)(2,1)} %param.10) | copy-start | bytes 196612
  11.2 7.4 %copy-start.4 = (bf16[16,32,256]{2,1,0:T(8,128)(2,1)S(1)}, bf16[16,32,256]{2,1,0:T(8,128)(2,1)}, u32[]{:S(2)}) copy-start(bf16[16,32,256]{2,1,0:T(8,128)(2,1)} %param.13) | copy-start | bytes 786436
  11.2 10.4 %copy-start.19 = (bf16[256]{0:T(256)(128)(2,1)S(1)}, bf16[256]{0:T(256)(128)(2,1)}, u32[]{:S(2)}) copy-start(bf16[256]{0:T(256)(128)(2,1)} %param.11) | copy-start | bytes 1540
  11.2 35.1 %all-to-all-start = ((bf16[32,144,128]{2,1,0:T(8,128)(2,1)}), bf16[32,144,128]{2,1,0:T(8,128)(2,1)S(1)}, u32[]{:S(2)}, u32[]{:S(2)}) async-start(bf16[32,144,128]{2,1,0:T(8,128)(2,1)} %pad_maximum_fusion.5), calls=%async_computation | async-start | bytes 2359296 | tf_op jit(solution)/shard_map/all_to_all | solution.py:87
  18.5 264.7 %all-reduce.7.cloned.1.call-start = ((), (), s32[]{:S(2)}) async-start(), calls=%async_computation.5 | async-start | bytes 14417920
  18.6 7.5 %collective-permute-start.5 = (bf16[16,3,256]{2,1,0:T(4,128)(2,1)S(1)}, bf16[16,3,256]{2,1,0:T(4,128)(2,1)S(1)}, u32[]{:S(2)}, u32[]{:S(2)}) collective-permute-start(bf16[16,3,256]{2,1,0:T(4,128)(2,1)S(1)} %get-tuple-element.22), channel_id=1, source_target_pairs={{0,28},{4,0},{8,4},{12,8},{16,12},{20,16},{24,20},{28,24},{1,29},{... | collective-permute-start | bytes 73736 | tf_op jit(solution)/shard_map/ppermute | solution.py:26
  21.1 7.8 %collective-permute-start.4 = (bf16[16,3,256]{2,1,0:T(4,128)(2,1)S(1)}, bf16[16,3,256]{2,1,0:T(4,128)(2,1)S(1)}, u32[]{:S(2)}, u32[]{:S(2)}) collective-permute-start(bf16[16,3,256]{2,1,0:T(4,128)(2,1)S(1)} %get-tuple-element.21), channel_id=1, source_target_pairs={{0,4},{4,8},{8,12},{12,16},{16,20},{20,24},{24,28},{28,0},{1,5},{5... | collective-permute-start | bytes 73736 | tf_op jit(solution)/shard_map/ppermute | solution.py:25
  21.6 43.7 %copy-start.14 = (pred[22]{0:T(512)(128)(4,1)}, pred[22]{0:T(512)(128)(4,1)S(1)}, u32[]{:S(2)}) copy-start(pred[22]{0:T(512)(128)(4,1)S(1)} %compare_and_fusion.4) | copy-start | bytes 70
  50.4 9.0 %copy-start.8 = (bf16[512,128]{1,0:T(8,128)(2,1)}, bf16[512,128]{1,0:T(8,128)(2,1)S(1)}, u32[]{:S(2)}) copy-start(bf16[512,128]{1,0:T(8,128)(2,1)S(1)} %fusion.19) | copy-start | bytes 393220
  50.7 8.6 %collective-permute-start.1 = (bf16[16,6,256]{2,1,0:T(8,128)(2,1)S(1)}, bf16[16,6,256]{2,1,0:T(8,128)(2,1)S(1)}, u32[]{:S(2)}, u32[]{:S(2)}) collective-permute-start(bf16[16,6,256]{2,1,0:T(8,128)(2,1)S(1)} %get-tuple-element.24), channel_id=1, source_target_pairs={{0,28},{4,0},{8,4},{12,8},{16,12},{20,16},{24,20},{28,24},{1,29},{... | collective-permute-start | bytes 147464 | tf_op jit(solution)/shard_map/ppermute | solution.py:26
  53.4 5.9 %collective-permute-start = (bf16[16,6,256]{2,1,0:T(8,128)(2,1)S(1)}, bf16[16,6,256]{2,1,0:T(8,128)(2,1)S(1)}, u32[]{:S(2)}, u32[]{:S(2)}) collective-permute-start(bf16[16,6,256]{2,1,0:T(8,128)(2,1)S(1)} %get-tuple-element.23), channel_id=1, source_target_pairs={{0,4},{4,8},{8,12},{12,16},{16,20},{20,24},{24,28},{28,0},{1,5},{5... | collective-permute-start | bytes 147464 | tf_op jit(solution)/shard_map/ppermute | solution.py:25
  53.4 12.5 %collective-permute-start.7 = (bf16[3,38,256]{2,1,0:T(8,128)(2,1)S(1)}, bf16[3,38,256]{2,1,0:T(8,128)(2,1)S(1)}, u32[]{:S(2)}, u32[]{:S(2)}) collective-permute-start(bf16[3,38,256]{2,1,0:T(8,128)(2,1)S(1)} %get-tuple-element.20), channel_id=1, source_target_pairs={{1,0},{2,1},{3,2},{5,4},{6,5},{7,6},{9,8},{10,9},{11,10},{13,12},{... | collective-permute-start | bytes 175112 | tf_op jit(solution)/shard_map/ppermute | solution.py:29
  54.7 11.2 %collective-permute-start.6 = (bf16[3,38,256]{2,1,0:T(8,128)(2,1)S(1)}, bf16[3,38,256]{2,1,0:T(8,128)(2,1)S(1)}, u32[]{:S(2)}, u32[]{:S(2)}) collective-permute-start(bf16[3,38,256]{2,1,0:T(8,128)(2,1)S(1)} %get-tuple-element.19), channel_id=1, source_target_pairs={{0,1},{1,2},{2,3},{4,5},{5,6},{6,7},{8,9},{9,10},{10,11},{12,13},{... | collective-permute-start | bytes 175112 | tf_op jit(solution)/shard_map/ppermute | solution.py:28
  59.3 9.2 %copy-start.6 = (bf16[16,6,256]{2,1,0:T(8,128)(2,1)}, bf16[16,6,256]{2,1,0:T(8,128)(2,1)S(1)}, u32[]{:S(2)}) copy-start(bf16[16,6,256]{2,1,0:T(8,128)(2,1)S(1)} %collective-permute-done) | copy-start | bytes 147460
  59.5 7.7 %collective-permute-start.3 = (bf16[6,44,256]{2,1,0:T(8,128)(2,1)S(1)}, bf16[6,44,256]{2,1,0:T(8,128)(2,1)S(1)}, u32[]{:S(2)}, u32[]{:S(2)}) collective-permute-start(bf16[6,44,256]{2,1,0:T(8,128)(2,1)S(1)} %get-tuple-element.16), channel_id=1, source_target_pairs={{1,0},{2,1},{3,2},{5,4},{6,5},{7,6},{9,8},{10,9},{11,10},{13,12},{... | collective-permute-start | bytes 405512 | tf_op jit(solution)/shard_map/ppermute | solution.py:29
  60.8 7.6 %collective-permute-start.2 = (bf16[6,44,256]{2,1,0:T(8,128)(2,1)S(1)}, bf16[6,44,256]{2,1,0:T(8,128)(2,1)S(1)}, u32[]{:S(2)}, u32[]{:S(2)}) collective-permute-start(bf16[6,44,256]{2,1,0:T(8,128)(2,1)S(1)} %get-tuple-element.15), channel_id=1, source_target_pairs={{0,1},{1,2},{2,3},{4,5},{5,6},{6,7},{8,9},{9,10},{10,11},{12,13},{... | collective-permute-start | bytes 405512 | tf_op jit(solution)/shard_map/ppermute | solution.py:28
  65.9 2.9 copy-start.10
  65.9 2.9 copy-start.12
  68.4 0.7 copy-start.2
  69.0 0.7 copy-start.25
  73.3 1.1 copy-start.16
  75.9 1.7 copy-start.24
  81.2 2.0 copy-start.18
  81.9 1.3 copy-start.23
  85.3 1.0 copy-start.1
  85.3 1.0 copy-start.17
  90.6 1.0 copy-start.5
  90.7 1.0 copy-start.11
  90.7 1.0 copy-start.13
  90.7 1.0 copy-start.15
  92.0 0.7 copy-start.22
  98.2 0.7 copy-start.21
  100.2 0.9 copy-start.3
  100.3 0.9 copy-start.7
  109.6 0.7 copy-start.20
  111.5 0.9 copy-start.9
  116.8 227.8 %all-gather.8.cloned.1.call-start = ((), (), s32[]{:S(2)}) async-start(), calls=%async_computation.4 | async-start | bytes 1216512 | tf_op jit(solution)/shard_map/all_gather | solution.py:174
  284.8 116.6 %all-gather.6.cloned.1.call-start = ((), (), s32[]{:S(2)}) async-start(), calls=%async_computation.3 | async-start | bytes 1216512 | tf_op jit(solution)/shard_map/all_gather | solution.py:174
  286.4 172.0 %all-gather.4.cloned.1.call-start = ((), (), s32[]{:S(2)}) async-start(), calls=%async_computation.2 | async-start | bytes 1284096 | tf_op jit(solution)/shard_map/all_gather | solution.py:174
  460.7 3.0 slice-start
Sparse Core Ops, SparseCore 0:
  116.9 166.2 all-reduce.6
  287.0 57.5 all-gather.7
  348.3 53.0 all-gather.5
  405.2 53.1 all-gather.3
